TPU v7x, 512 devices: a whole 4x8x8 slice. The times are simulated.
512 devices in a mesh: grp: 8 (over z_hi, core), req: 64 (over y, x, z_lo).
Axes of the slice: x: 4, y: 8, z: 8 (z_hi: 4, z_lo: 2; z = z_hi * 2 + z_lo), core: 2. Of those that a mesh axis runs over, the one named last changes fastest.
Arguments:
- queries: bfloat16 [8, 64, 4, 2048], P('grp', 'req'), may hold values from -12 to 1700
- suffix_kv: bfloat16 [8, 64, 2, 4, 512], P('grp', 'req'), may hold values from -6 to 6
- prefix_pool: bfloat16 [8, 64, 3, 2, 128, 512], P('grp', 'req'), may hold values from -6 to 6
- page_table: int32 [64, 16], P('req'), may hold values from 0 to 23, as said below
- suffix_len: int32 [8, 64], P('grp'), may hold values from 1 to 4, 128 in all within a row
- residual: bfloat16 [8, 256, 4096], P('grp', None, 'req'), may hold values from -40 to 40
- out_weight: bfloat16 [2048, 4096], P(None, 'req'), may hold values from -0.5 to 0.5
- norm_gain: bfloat16 [4096], P('req'), may hold values from 0.099609375 to 1.8984375
- gate_up: bfloat16 [2, 4096, 8192], P(None, None, 'req'), may hold values from -0.09375 to 0.09375
- down_weight: bfloat16 [8192, 4096], P('req'), may hold values from -0.1875 to 0.1875
Outputs:
- hidden_out: bfloat16 [8, 256, 4096], P('grp', None, 'req')
Inputs may be any that keep to these rules, and one draw needn't show every extreme that they name: `page_table`: row b lists 16 different pages of group b's pool; pool page p is slot p % 3 on the member p // 3.
All inputs are finite; a program needn't handle non-finite values.
Results may differ from a plain program's by a relative error of at most 0.028.
Values may be sent and summed in bfloat16 or wider, within the bound.
No kernel may reach another device: no remote copies, remote signals or barrier semaphores. Data moves between devices by JAX's collectives and lax.ppermute only.
A program may use at most 64 MiB of HBM per device.

v0:
```python
import jax
import jax.numpy as jnp
from jax import lax
from jax.sharding import PartitionSpec as P

D = 4096
HD = 128
QH = 16
KVH = 4
PAGE = 128


def split_heads(query_rows):
    row_count = query_rows.shape[0]
    query_heads = query_rows.reshape(row_count, KVH, QH // KVH, HD)
    return jnp.transpose(query_heads, (1, 2, 0, 3))


def empty_state(row_count):
    running_max = jnp.full((KVH, QH // KVH, row_count), -1e30, jnp.float32)
    weight_sum = jnp.zeros((KVH, QH // KVH, row_count), jnp.float32)
    accumulated = jnp.zeros((KVH, QH // KVH, row_count, HD), jnp.float32)
    return (running_max, weight_sum, accumulated)


def page_block(softmax_state, pages_part, query_heads, table_row):
    running_max, weight_sum, accumulated = softmax_state
    page_count = pages_part.shape[0]
    page_index = jnp.arange(page_count, dtype=jnp.int32)
    page_used = jnp.any(page_index[:, None] == table_row[None, :], axis=1)
    token_live = jnp.repeat(page_used, PAGE)
    key_rows = pages_part[:, 0].reshape(page_count * PAGE, KVH, HD)
    value_rows = pages_part[:, 1].reshape(page_count * PAGE, KVH, HD)
    scores = jnp.einsum(
        "jgsd,tjd->jgst", query_heads, key_rows, preferred_element_type=jnp.float32
    ) * HD ** (-0.5)
    scores = jnp.where(token_live, scores, -1e30)
    merged_max = jnp.maximum(running_max, jnp.max(scores, axis=-1))
    weights = jnp.where(token_live, jnp.exp(scores - merged_max[..., None]), 0.0)
    weight_sum = jnp.sum(weights, axis=-1)
    weighted = jnp.einsum(
        "jgst,tjd->jgsd",
        weights.astype(jnp.bfloat16),
        value_rows,
        preferred_element_type=jnp.float32,
    )
    accumulated = weighted
    return (merged_max, weight_sum, accumulated)


def with_suffix(softmax_state, query_heads, own_suffix):
    running_max, weight_sum, accumulated = softmax_state
    row_count = query_heads.shape[2]
    key_rows = own_suffix[0].reshape(row_count, KVH, HD)
    value_rows = own_suffix[1].reshape(row_count, KVH, HD)
    scores = jnp.einsum(
        "jgsd,tjd->jgst", query_heads, key_rows, preferred_element_type=jnp.float32
    ) * HD ** (-0.5)
    causal = jnp.arange(row_count)[:, None] >= jnp.arange(row_count)[None, :]
    scores = jnp.where(causal, scores, -1e30)
    merged_max = jnp.maximum(running_max, jnp.max(scores, axis=-1))
    weights = jnp.where(causal, jnp.exp(scores - merged_max[..., None]), 0.0)
    rescale = jnp.exp(running_max - merged_max)
    weight_sum = weight_sum * rescale + jnp.sum(weights, axis=-1)
    weighted = jnp.einsum(
        "jgst,tjd->jgsd",
        weights.astype(jnp.bfloat16),
        value_rows,
        preferred_element_type=jnp.float32,
    )
    accumulated = accumulated * rescale[..., None] + weighted
    accumulated = accumulated / weight_sum[..., None]
    ordered = jnp.transpose(accumulated, (2, 0, 1, 3))
    return ordered.reshape(row_count, QH * HD).astype(jnp.bfloat16)


def body(
    queries,
    suffix_kv,
    prefix_pool,
    page_table,
    suffix_len,
    residual,
    out_weight,
    norm_gain,
    gate_up,
    down_weight,
):
    slot_count = queries.shape[2]
    own_queries = queries[0, 0]
    own_pool = prefix_pool[0, 0]
    table_row = page_table[0]
    own_heads = split_heads(own_queries)
    softmax_state = page_block(
        empty_state(slot_count),
        lax.all_gather(own_pool, "grp", axis=0, tiled=True),
        own_heads,
        table_row,
    )
    attention = with_suffix(softmax_state, own_heads, suffix_kv[0, 0])
    projected = jnp.dot(
        lax.all_gather(attention, "req", axis=0, tiled=True),
        out_weight,
        preferred_element_type=jnp.float32,
    )
    stream = (residual[0].astype(jnp.float32) + projected).astype(jnp.bfloat16)
    wide_local = stream.astype(jnp.float32)
    partial_sq = jnp.sum(wide_local * wide_local, axis=1)
    row_sumsq = lax.psum(partial_sq, "req")
    inverse_rms = lax.rsqrt(row_sumsq / D + 1e-05)
    normed = (wide_local * inverse_rms[:, None] * norm_gain.astype(jnp.float32)[None, :]).astype(
        jnp.bfloat16
    )
    gate_up_out = jnp.einsum(
        "nc,kcf->knf",
        lax.all_gather(normed, "req", axis=1, tiled=True),
        gate_up,
        preferred_element_type=jnp.float32,
    )
    hidden = (jax.nn.silu(gate_up_out[0]) * gate_up_out[1]).astype(jnp.bfloat16)
    partial_value = jnp.dot(hidden, down_weight, preferred_element_type=jnp.float32)
    summed = lax.psum_scatter(partial_value, "req", scatter_dimension=1, tiled=True)
    lengths = suffix_len[0]
    slot_index = jnp.arange(stream.shape[0], dtype=jnp.int32) % slot_count
    slot_live = (slot_index < jnp.repeat(lengths, slot_count)).astype(jnp.float32)
    result_rows = (wide_local + summed) * slot_live[:, None]
    return result_rows.astype(jnp.bfloat16)[None]


def solution(mesh):
    return jax.shard_map(
        body,
        mesh=mesh,
        in_specs=(
            P("grp", "req", None, None),
            P("grp", "req", None, None, None),
            P("grp", "req", None, None, None, None),
            P("req", None),
            P("grp", None),
            P("grp", None, "req"),
            P(None, "req"),
            P("req"),
            P(None, None, "req"),
            P("req", None),
        ),
        out_specs=P("grp", None, "req"),
        check_vma=False,
    )
```

profile of v0, /device:TPU:128, one launch (start us, length us, event | category | flops | bytes accessed | tf_op | source)
XLA Modules:
  0.0 1206.9 jit_solution(9325458423505003093)
XLA Ops:
  6.5 0.0 copy-start
  6.5 0.0 all-gather.8.cloned.1.call-start
  6.5 0.7 all-gather.8.cloned.1.call-update
  7.3 0.0 all-gather.10.cloned.1.call-start
  7.3 0.7 fusion.46
  8.1 0.1 broadcast_bitcast_fusion
  8.1 1.0 fusion.58
  9.1 76.7 %all-gather.8.cloned.1.call-done = bf16[1,1,24,2,128,512]{5,4,3,1,0,2:T(8,128)(2,1)} async-done(((bf16[1,1,3,2,128,512]{5,4,3,1,0,2:T(8,128)(2,1)}), bf16[1,1,24,2,128,512]{5,4,3,1,0,2:T(8,128)(2,1)}) %all-gather.8.cloned.1.call-update) | async-done | bytes 6291472 | tf_op jit(solution)/shard_map/all_gather | solution.py:96
  85.8 6.2 fusion.56
  92.0 0.0 copy-start.5
  92.0 5.5 reshape.67
  97.5 0.0 copy-start.6
  97.5 0.0 copy-done.5
  97.5 2.9 fusion.57
  100.5 0.0 copy-done.6
  100.5 0.2 convolution_bitcast_fusion
  100.7 5.5 reshape.68
  106.2 0.0 copy-start.7
  106.2 0.5 fusion.27
  106.7 0.0 copy-start.2
  106.8 0.0 copy-start.3
  106.8 3.4 fusion.24
  110.2 0.0 all-gather.10.cloned.1.call-update
  110.2 0.0 all-gather.6.cloned.1.call-start
  110.2 0.0 copy-done.7
  110.3 299.2 %all-gather.10.cloned.1.call-done = bf16[64,4,2048]{2,1,0:T(4,128)(2,1)} async-done(((bf16[1,4,2048]{2,1,0:T(4,128)(2,1)}), bf16[64,4,2048]{2,1,0:T(4,128)(2,1)}) %all-gather.10.cloned.1.call-update) | async-done | bytes 1048592 | tf_op jit(solution)/shard_map/all_gather | solution.py:102
  409.4 1.3 reshape.60
  410.8 0.0 copy-done.2
  410.8 0.0 copy-done.3
  410.8 0.5 multiply_reduce_fusion
  411.3 156.7 %psum.7 = f32[256]{0:T(256)S(1)} all-reduce(f32[256]{0:T(256)S(1)} %get-tuple-element.15), channel_id=1, replica_groups=mesh['grp'=8,'req'=64] {'req'}, use_global_device_ids=true, to_apply=%region_6.7 | all-reduce | flops 256 | bytes 2048 | tf_op jit(solution)/shard_map/psum | solution.py:109
  568.0 0.7 multiply_convert_fusion.1
  568.7 0.0 all-gather.6.cloned.1.call-update
  568.7 0.0 copy-start.1
  568.7 0.0 reduce-scatter.2.cloned.1.call-start
  568.7 298.6 %all-gather.6.cloned.1.call-done = bf16[256,4096]{0,1:T(8,128)(2,1)} async-done(((bf16[256,64]{0,1:T(8,128)(2,1)}), bf16[256,4096]{0,1:T(8,128)(2,1)}) %all-gather.6.cloned.1.call-update) | async-done | bytes 2097168 | tf_op jit(solution)/shard_map/all_gather | solution.py:116
  867.4 0.0 copy-done
  867.4 2.3 fusion.6
  869.7 0.0 copy-done.1
  869.7 2.7 fusion.35
  872.4 0.0 copy-start.4
  872.4 0.0 reduce-scatter.2.cloned.1.call-update
  872.4 0.6 copy-done.4
  873.1 0.1 broadcast_in_dim.56
  873.1 0.1 reshape.56
  873.3 325.7 %reduce-scatter.2.cloned.1.call-done = f32[256,64]{0,1:T(8,128)} async-done(((f32[256,4096]{0,1:T(8,128)}), f32[256,64]{0,1:T(8,128)}) %reduce-scatter.2.cloned.1.call-update) | async-done | bytes 65552 | tf_op jit(solution)/shard_map/reduce_scatter | solution.py:122
  1199.0 1.5 fusion.38
  (7 shorter events, 0.1 us)
Async XLA Ops:
  6.5 860.8 %copy-start = (bf16[2,4096,128]{2,1,0:T(8,128)(2,1)S(1)}, bf16[2,4096,128]{2,1,0:T(8,128)(2,1)}, u32[]{:S(2)}) copy-start(bf16[2,4096,128]{2,1,0:T(8,128)(2,1)} %param.18) | copy-start | bytes 6291460
  6.5 79.3 %all-gather.8.cloned.1.call-start = ((), (), s32[]{:S(2)}) async-start(), calls=%async_computation.3 | async-start | bytes 7077888 | tf_op jit(solution)/shard_map/all_gather | solution.py:96
  7.3 402.2 %all-gather.10.cloned.1.call-start = ((), (), s32[]{:S(2)}) async-start(), calls=%async_computation.4 | async-start | bytes 1064960 | tf_op jit(solution)/shard_map/all_gather | solution.py:102
  92.0 5.5 copy-start.5
  97.5 3.0 copy-start.6
  106.2 4.0 copy-start.7
  106.7 304.1 %copy-start.2 = (bf16[2048,64]{0,1:T(8,128)(2,1)S(1)}, bf16[2048,64]{0,1:T(8,128)(2,1)}, u32[]{:S(2)}) copy-start(bf16[2048,64]{0,1:T(8,128)(2,1)} %param.16) | copy-start | bytes 786436
  106.8 304.1 %copy-start.3 = (bf16[1,256,64]{1,2,0:T(8,128)(2,1)S(1)}, bf16[1,256,64]{1,2,0:T(8,128)(2,1)}, u32[]{:S(2)}) copy-start(bf16[1,256,64]{1,2,0:T(8,128)(2,1)} %param.15) | copy-start | bytes 98308
  110.2 757.2 %all-gather.6.cloned.1.call-start = ((), (), s32[]{:S(2)}) async-start(), calls=%async_computation.1 | async-start | bytes 2129920 | tf_op jit(solution)/shard_map/all_gather | solution.py:116
  568.7 301.0 %copy-start.1 = (bf16[128,4096]{1,0:T(8,128)(2,1)S(1)}, bf16[128,4096]{1,0:T(8,128)(2,1)}, u32[]{:S(2)}) copy-start(bf16[128,4096]{1,0:T(8,128)(2,1)} %param.19) | copy-start | bytes 3145732
  568.7 630.3 %reduce-scatter.2.cloned.1.call-start = ((), (), s32[]{:S(2)}) async-start(), calls=%async_computation.2 | async-start | bytes 4259840 | tf_op jit(solution)/shard_map/reduce_scatter | solution.py:122
  872.4 0.7 copy-start.4
Sparse Core Ops, SparseCore 0:
  9.5 76.3 all-gather.7
  110.3 299.0 all-gather.9
  568.8 298.5 all-gather.5
  872.6 326.3 reduce-scatter.1
where the time goes:
time: 1210 us
  waiting for transfers between devices  1000 us (83%)
  blocking collectives  157 us (13%)
  local copies, waits for them, and re-layouts  19.5 us (2%)
  between operations  13.3 us (1%)
  matrix products  13 us (1%)
    reduce_scatter x1, waiting for transfers between devices, body(): lax.psum_scatter(partial_value, 'req', scatter_dimension=1, tiled=True)  326 us
    all_gather x1, waiting for transfers between devices, body(): lax.all_gather(attention, 'req', axis=0, tiled=True)  299 us
    all_gather x1, waiting for transfers between devices, body(): lax.all_gather(normed, 'req', axis=1, tiled=True)  299 us
    psum x1, blocking collectives, body(): row_sumsq = lax.psum(partial_sq, 'req')  157 us
    all_gather x1, waiting for transfers between devices, body(): lax.all_gather(own_pool, 'grp', axis=0, tiled=True)  76.7 us
  transfers between devices with their start and end apart: 4, of which 4 were waited for; matrix products, arithmetic and copies ran while one was open for 0% of the time, Pallas kernels for 0%

commit v1 on v0

--- a/solution.py
+++ b/solution.py
@@ -93,7 +93,15 @@
     own_heads = split_heads(own_queries)
     softmax_state = page_block(
         empty_state(slot_count),
-        lax.all_gather(own_pool, "grp", axis=0, tiled=True),
+        jnp.concatenate(
+            lax.all_to_all(
+                jnp.stack(lax.axis_size("grp") * [own_pool]),
+                concat_axis=0,
+                axis_name="grp",
+                split_axis=0,
+            ),
+            axis=0,
+        ),
         own_heads,
         table_row,
     )

time: 1210 us -> 1280 us (1.058)
  waiting for transfers between devices: 1000 us -> 1060 us
    all_to_all x0 -> x1, waiting for transfers between devices: none -> 118 us  [body(): lax.all_to_all(jnp.stack(lax.axis_size('grp') * [own_pool]), concat_axis=...]
    all_gather x1 -> x0, waiting for transfers between devices: 76.7 us -> none  [body(): lax.all_gather(own_pool, 'grp', axis=0, tiled=True)]
    all_gather x1, waiting for transfers between devices: 299 us -> 321 us  [body(): lax.all_gather(attention, 'req', axis=0, tiled=True)]
where the time goes in v1:
time: 1280 us
  waiting for transfers between devices  1060 us (83%)
  blocking collectives  157 us (12%)
  local copies, waits for them, and re-layouts  24.2 us (2%)
  between operations  13.2 us (1%)
    reduce_scatter x1, waiting for transfers between devices, body(): lax.psum_scatter(partial_value, 'req', scatter_dimension=1, tiled=True)  325 us
    all_gather x1, waiting for transfers between devices, body(): lax.all_gather(attention, 'req', axis=0, tiled=True)  321 us
    all_gather x1, waiting for transfers between devices, body(): lax.all_gather(normed, 'req', axis=1, tiled=True)  299 us
    psum x1, blocking collectives, body(): row_sumsq = lax.psum(partial_sq, 'req')  157 us
    all_to_all x1, waiting for transfers between devices, body(): lax.all_to_all(jnp.stack(lax.axis_size('grp') * [own_pool]), concat_axis=...  118 us
  transfers between devices with their start and end apart: 4, of which 4 were waited for; matrix products, arithmetic and copies ran while one was open for 0% of the time, Pallas kernels for 0%

profile of v1, /device:TPU:128, one launch (start us, length us, event | category | flops | bytes accessed | tf_op | source)
XLA Modules:
  0.0 1281.1 jit_solution(2650842302263137617)
XLA Ops:
  6.5 0.0 copy-start
  6.5 4.7 stack.3
  11.2 0.0 copy-start.7
  11.2 0.0 copy-start.5
  11.2 0.0 copy-start.6
  11.2 9.2 all-to-all-start
  20.4 0.0 all-gather.6.cloned.1.call-start
  20.4 0.0 copy-done.7
  20.4 0.1 fusion.46
  20.5 0.1 broadcast_bitcast_fusion
  20.6 0.0 copy-done.5
  20.6 0.0 copy-done.6
  20.6 0.3 fusion.58
  20.9 117.6 %all-to-all-done = bf16[8,3,2,128,512]{4,3,2,1,0:T(8,128)(2,1)} async-done(((bf16[8,3,2,128,512]{4,3,2,1,0:T(8,128)(2,1)}), bf16[8,3,2,128,512]{4,3,2,1,0:T(8,128)(2,1)}, u32[]{:S(2)}, u32[]{:S(2)}) %all-to-all-start) | async-done | bytes 6291488 | tf_op jit(solution)/shard_map/all_to_all | solution.py:97
  138.4 6.2 fusion.56
  144.7 5.5 reshape.72
  150.2 2.9 fusion.57
  153.1 0.2 convolution_bitcast_fusion
  153.3 5.5 reshape.73
  158.8 0.0 copy-start.8
  158.8 0.5 fusion.27
  159.3 0.0 copy-start.2
  159.4 0.0 copy-start.3
  159.4 3.4 fusion.24
  162.8 0.0 all-gather.6.cloned.1.call-update
  162.8 0.0 all-gather.4.cloned.1.call-start
  162.8 0.0 copy-done.8
  162.9 320.9 %all-gather.6.cloned.1.call-done = bf16[64,4,2048]{2,1,0:T(4,128)(2,1)} async-done(((bf16[1,4,2048]{2,1,0:T(4,128)(2,1)}), bf16[64,4,2048]{2,1,0:T(4,128)(2,1)}) %all-gather.6.cloned.1.call-update) | async-done | bytes 1048592 | tf_op jit(solution)/shard_map/all_gather | solution.py:110
  483.8 1.3 reshape.65
  485.1 0.0 copy-done.2
  485.1 0.0 copy-done.3
  485.1 0.5 multiply_reduce_fusion
  485.6 156.7 %psum.7 = f32[256]{0:T(256)S(1)} all-reduce(f32[256]{0:T(256)S(1)} %get-tuple-element.15), channel_id=1, replica_groups=mesh['grp'=8,'req'=64] {'req'}, use_global_device_ids=true, to_apply=%region_6.7 | all-reduce | flops 256 | bytes 2048 | tf_op jit(solution)/shard_map/psum | solution.py:117
  642.3 0.7 multiply_convert_fusion.1
  643.0 0.0 all-gather.4.cloned.1.call-update
  643.0 0.0 copy-start.1
  643.0 0.0 reduce-scatter.2.cloned.1.call-start
  643.1 298.6 %all-gather.4.cloned.1.call-done = bf16[256,4096]{0,1:T(8,128)(2,1)} async-done(((bf16[256,64]{0,1:T(8,128)(2,1)}), bf16[256,4096]{0,1:T(8,128)(2,1)}) %all-gather.4.cloned.1.call-update) | async-done | bytes 2097168 | tf_op jit(solution)/shard_map/all_gather | solution.py:124
  941.7 0.0 copy-done
  941.7 2.3 fusion.6
  944.0 0.0 copy-done.1
  944.0 2.7 fusion.35
  946.7 0.0 copy-start.4
  946.7 0.0 reduce-scatter.2.cloned.1.call-update
  946.8 0.6 copy-done.4
  947.4 0.1 broadcast_in_dim.56
  947.5 0.1 reshape.62
  947.6 325.5 %reduce-scatter.2.cloned.1.call-done = f32[256,64]{0,1:T(8,128)} async-done(((f32[256,4096]{0,1:T(8,128)}), f32[256,64]{0,1:T(8,128)}) %reduce-scatter.2.cloned.1.call-update) | async-done | bytes 65552 | tf_op jit(solution)/shard_map/reduce_scatter | solution.py:130
  1273.1 1.5 fusion.38
  (7 shorter events, 0.1 us)
Async XLA Ops:
  6.5 935.2 %copy-start = (bf16[2,4096,128]{2,1,0:T(8,128)(2,1)S(1)}, bf16[2,4096,128]{2,1,0:T(8,128)(2,1)}, u32[]{:S(2)}) copy-start(bf16[2,4096,128]{2,1,0:T(8,128)(2,1)} %param.18) | copy-start | bytes 6291460
  11.2 9.2 copy-start.7
  11.2 9.4 copy-start.5
  11.2 9.4 copy-start.6
  11.2 127.2 %all-to-all-start = ((bf16[8,3,2,128,512]{4,3,2,1,0:T(8,128)(2,1)}), bf16[8,3,2,128,512]{4,3,2,1,0:T(8,128)(2,1)}, u32[]{:S(2)}, u32[]{:S(2)}) async-start(bf16[8,3,2,128,512]{4,3,2,1,0:T(8,128)(2,1)} %stack.3), calls=%async_computation | async-start | bytes 12582912 | tf_op jit(solution)/shard_map/all_to_all | solution.py:97
  20.4 463.4 %all-gather.6.cloned.1.call-start = ((), (), s32[]{:S(2)}) async-start(), calls=%async_computation.4 | async-start | bytes 1064960 | tf_op jit(solution)/shard_map/all_gather | solution.py:110
  158.8 4.0 copy-start.8
  159.3 325.8 %copy-start.2 = (bf16[2048,64]{0,1:T(8,128)(2,1)S(1)}, bf16[2048,64]{0,1:T(8,128)(2,1)}, u32[]{:S(2)}) copy-start(bf16[2048,64]{0,1:T(8,128)(2,1)} %param.16) | copy-start | bytes 786436
  159.4 325.8 %copy-start.3 = (bf16[1,256,64]{1,2,0:T(8,128)(2,1)S(1)}, bf16[1,256,64]{1,2,0:T(8,128)(2,1)}, u32[]{:S(2)}) copy-start(bf16[1,256,64]{1,2,0:T(8,128)(2,1)} %param.15) | copy-start | bytes 98308
  162.8 778.9 %all-gather.4.cloned.1.call-start = ((), (), s32[]{:S(2)}) async-start(), calls=%async_computation.2 | async-start | bytes 2129920 | tf_op jit(solution)/shard_map/all_gather | solution.py:124
  643.0 301.0 %copy-start.1 = (bf16[128,4096]{1,0:T(8,128)(2,1)S(1)}, bf16[128,4096]{1,0:T(8,128)(2,1)}, u32[]{:S(2)}) copy-start(bf16[128,4096]{1,0:T(8,128)(2,1)} %param.19) | copy-start | bytes 3145732
  643.0 630.1 %reduce-scatter.2.cloned.1.call-start = ((), (), s32[]{:S(2)}) async-start(), calls=%async_computation.3 | async-start | bytes 4259840 | tf_op jit(solution)/shard_map/reduce_scatter | solution.py:130
  946.7 0.7 copy-start.4
Sparse Core Ops, SparseCore 0:
  162.9 320.8 all-gather.5
  643.1 298.5 all-gather.3
  946.9 326.1 reduce-scatter.1
